TPU v7x, 256 devices: a whole 4x4x8 slice. The times are simulated.
256 devices in a mesh: cent: 8 (over z), dp: 32 (over x, y, core).
Axes of the slice: x: 4, y: 4, z: 8, core: 2. Of those that a mesh axis runs over, the one named last changes fastest.
Arguments:
- points: bfloat16 [32768, 1024], P('dp'), may hold values from -6 to 6
- cluster_ids: int32 [32768, 1], P('dp'), may hold values from 0 to 63; in each aligned block of 1024 rows (0 to 1023, 1024 to 2047, ...) at most 64 rows name the same one
- centroids: bfloat16 [8192, 1024], P('cent'), may hold values from -6 to 6
- sub_centroids: bfloat16 [64, 1024, 1024], P('dp', 'cent'), may hold values from -6 to 6
Outputs:
- assign: bfloat16 [32768, 8192], P('dp', 'cent')
- sub_assign: bfloat16 [32768, 1024], P('dp', 'cent')
Inputs may be any that keep to these rules, and one draw needn't show every extreme that they name: `cluster_ids`: among the 1024 points of one index of dp, no level-two cluster holds more than 64 points; some cluster holds exactly 64 in some block.
All inputs are finite; a program needn't handle non-finite values.
Results may differ from a plain program's by a relative error of at most 0.001.
Values may be sent and summed in bfloat16 or wider, within the bound.
No kernel may reach another device: no remote copies, remote signals or barrier semaphores. Data moves between devices by JAX's collectives and lax.ppermute only.
A program may use at most 128 MiB of HBM per device.

v0:
```python
import jax
import jax.numpy as jnp
from jax import lax
from jax.sharding import PartitionSpec as P

CAP = 64
ITERS = 3
EPS = 1e-06
TAU = 0.05


def inverse_norm(rows):
    values = rows.astype(jnp.float32)
    return lax.rsqrt(jnp.mean(values * values, axis=-1) + EPS)


def shards(points, cluster_ids, centroids, sub_centroids):
    pts_count = points.shape[0]
    width = points.shape[1]
    dp_count = lax.axis_size("dp")
    cent_count = lax.axis_size("cent")
    group_dev = sub_centroids.shape[0]
    sub_dev = sub_centroids.shape[1]
    clusters = group_dev * dp_count
    total_cent = centroids.shape[0] * cent_count
    total_sub = sub_dev * cent_count
    inv_x = inverse_norm(points)
    inv_c = inverse_norm(centroids)
    inv_u = inverse_norm(sub_centroids)
    scores = jnp.einsum("pd,kd->pk", points, centroids, preferred_element_type=jnp.float32)
    expo = jnp.exp(scores * inv_x[:, None] * inv_c[None, :] * (1.0 / (width * TAU)))
    row_scale = jnp.ones((pts_count,), jnp.float32)
    col_scale = jnp.ones((centroids.shape[0],), jnp.float32)
    row_part = row_scale
    for step in range(ITERS):
        col_part = jnp.dot(row_scale, expo, precision=lax.Precision.HIGHEST)
        col_scale = 1.0 / lax.psum(col_part, "dp")
        row_part = jnp.dot(expo, col_scale, precision=lax.Precision.HIGHEST)
        if step + 1 < ITERS:
            row_scale = 1.0 / lax.psum(row_part, "cent")
    ids = cluster_ids[:, 0]
    labels = lax.broadcasted_iota(jnp.int32, (pts_count, clusters), 1)
    onehot = ids[:, None] == labels
    positions = lax.broadcasted_iota(jnp.int32, (pts_count, pts_count), 0)
    earlier = (positions > positions.T).astype(jnp.bfloat16)
    before = jnp.dot(earlier, onehot.astype(jnp.bfloat16), preferred_element_type=jnp.float32)
    rank = jnp.sum(before * onehot.astype(jnp.float32), axis=1).astype(jnp.int32)
    slot = ids * CAP + rank
    buffer = jnp.zeros((clusters * CAP, width), jnp.bfloat16).at[slot].set(points)
    scale_two = 1.0 / (width * TAU)
    outgoing = buffer.reshape(dp_count, group_dev * CAP, width)
    arrived = lax.all_to_all(outgoing, "dp", split_axis=0, concat_axis=0, tiled=True)
    arrived = arrived.reshape(dp_count, group_dev, CAP, width)
    inv_rows = inverse_norm(arrived)
    dots = jnp.einsum("sgcd,gkd->sgck", arrived, sub_centroids, preferred_element_type=jnp.float32)
    weights = jnp.exp(dots * inv_rows[..., None] * inv_u[None, :, None, :] * scale_two)
    weights = weights.reshape(dp_count, group_dev * CAP, sub_dev)
    returned = lax.all_to_all(weights, "dp", split_axis=0, concat_axis=0, tiled=True)
    slot_weights = returned.reshape(clusters * CAP, sub_dev)
    point_weights = slot_weights[slot]
    denom_part = jnp.sum(point_weights, axis=1)
    row_total = lax.psum(row_part, "cent")
    denominator = lax.psum(denom_part, "cent")
    row_scale = 1.0 / row_total
    assign = (expo * row_scale[:, None] * col_scale[None, :] * total_cent).astype(jnp.bfloat16)
    sub_assign = (total_sub * point_weights / denominator[:, None]).astype(jnp.bfloat16)
    return (assign, sub_assign)


def solution(mesh):
    return jax.shard_map(
        shards,
        mesh=mesh,
        in_specs=(P("dp", None), P("dp", None), P("cent", None), P("dp", "cent", None)),
        out_specs=(P("dp", "cent"), P("dp", "cent")),
        check_vma=False,
    )
```

profile of v0, /device:TPU:0, one launch (start us, length us, event | category | flops | bytes accessed | tf_op | source)
XLA Modules:
  0.0 412.9 jit_solution(17542967821555174308)
XLA Ops:
  0.6 1.4 fusion.11
  2.7 10.8 %scatter_custom_fusion = bf16[4096,1024]{1,0:T(8,128)(2,1)} fusion(s32[1024]{0:T(1024)S(1)} %bitcast.56, bf16[1024,1024]{1,0:T(8,128)(2,1)} %param.4, bf16[]{:T(256)} %constant.6.clone.1), kind=kCustom, calls=%fused_computation.6 | custom fusion | bytes 8389120 | tf_op jit(solution)/shard_map/scatter | solution.py:49
  13.5 6.1 %all-to-all-start = ((bf16[32,128,1024]{2,1,0:T(8,128)(2,1)}), bf16[32,128,1024]{2,1,0:T(8,128)(2,1)}, u32[]{:S(2)}, u32[]{:S(2)}) async-start(bf16[32,128,1024]{2,1,0:T(8,128)(2,1)} %bitcast.51), calls=%async_computation | async-start | bytes 16777216 | tf_op jit(solution)/shard_map/all_to_all | solution.py:52
  19.6 2.2 multiply_reduce_fusion.1
  22.3 2.6 multiply_exponential_fusion
  24.9 1.9 copy-done
  26.9 2.1 fusion.14
  28.9 141.6 %psum.49 = f32[1024]{0:T(1024)S(1)} all-reduce(f32[1024]{0:T(1024)S(1)} %bitcast.55), channel_id=1, replica_groups=mesh['cent'=8,'dp'=32] {'dp'}, use_global_device_ids=true, to_apply=%region_2.0 | all-reduce | flops 1024 | bytes 8192 | tf_op jit(solution)/shard_map/psum | solution.py:37
  170.5 5.8 %fusion.17 = f32[1,1024]{1,0:T(1,128)S(1)} fusion(f32[1024,1024]{1,0:T(8,128)} %copy-done, f32[1024,1]{0,1:T(1,128)S(1)} %bitcast.61), kind=kOutput, calls=%fused_computation.39 | convolution fusion | flops 12582912 | bytes 4202496 | tf_op jit(solution)/shard_map/dot_general | solution.py:38
  176.3 20.0 %psum.50 = f32[1024]{0:T(1024)S(1)} all-reduce(f32[1024]{0:T(1024)S(1)} %bitcast.62), channel_id=1, replica_groups=mesh['cent'=8,'dp'=32] {'cent'}, use_global_device_ids=true, to_apply=%region_3.0 | all-reduce | flops 1024 | bytes 8192 | tf_op jit(solution)/shard_map/psum | solution.py:40
  196.5 5.1 %multiply_reduce_fusion = f32[32,128]{1,0:T(8,128)S(1)} fusion(bf16[32,128,1024]{2,1,0:T(8,128)(2,1)} %all-to-all-done), kind=kLoop, calls=%fused_computation.2 | loop fusion | flops 12578816 | bytes 8404992 | tf_op jit(solution)/shard_map/reduce_sum | solution.py:14
  201.7 4.8 %fusion.7 = f32[32,2,64,128]{3,2,0,1:T(8,128)S(1)} fusion(bf16[32,2,64,1024]{3,2,1,0:T(8,128)(2,1)} %bitcast.16, f32[2,128]{1,0:T(2,128)S(1)} %add_rsqrt_fusion.3, f32[32,2,64]{2,0,1:T(8,128)S(1)} %copy.7, bf16[2,128,1024]{2,1,0:T(8,128)(2,1)S(1)} %copy-done.3), kind=kOutput, calls=%fused_computation.16 | convolution fusion | flops 1075314688 | bytes 11027456 | tf_op jit(solution)/shard_map/sgcd,gkd->sgck/dot_general | solution.py:55
  206.5 1.5 copy.8
  208.0 5.4 %all-to-all-start.1 = ((f32[32,128,128]{2,1,0:T(8,128)}), f32[32,128,128]{2,1,0:T(8,128)S(1)}, u32[]{:S(2)}, u32[]{:S(2)}) async-start(f32[32,128,128]{2,1,0:T(8,128)} %bitcast.53), calls=%async_computation.1 | async-start | bytes 4194304 | tf_op jit(solution)/shard_map/all_to_all | solution.py:58
  213.4 4.3 %fusion.18 = f32[1,1024]{1,0:T(1,128)S(1)} fusion(f32[1024,1]{0,1:T(1,128)S(1)} %bitcast.59, f32[1024,1024]{1,0:T(8,128)} %copy-done), kind=kOutput, calls=%fused_computation.40 | convolution fusion | flops 12582912 | bytes 4202496 | tf_op jit(solution)/shard_map/dot_general | solution.py:36
  217.6 78.1 %psum.51 = f32[1024]{0:T(1024)S(1)} all-reduce(f32[1024]{0:T(1024)S(1)} %bitcast.63), channel_id=1, replica_groups=mesh['cent'=8,'dp'=32] {'dp'}, use_global_device_ids=true, to_apply=%region_4.0 | all-reduce | flops 1024 | bytes 8192 | tf_op jit(solution)/shard_map/psum | solution.py:37
  295.7 5.8 %fusion.19 = f32[1,1024]{1,0:T(1,128)S(1)} fusion(f32[1024,1024]{1,0:T(8,128)} %copy-done, f32[1024,1]{0,1:T(1,128)S(1)} %bitcast.64), kind=kOutput, calls=%fused_computation.41 | convolution fusion | flops 12582912 | bytes 4202496 | tf_op jit(solution)/shard_map/dot_general | solution.py:38
  301.5 14.2 %psum.52 = f32[1024]{0:T(1024)S(1)} all-reduce(f32[1024]{0:T(1024)S(1)} %bitcast.65), channel_id=1, replica_groups=mesh['cent'=8,'dp'=32] {'cent'}, use_global_device_ids=true, to_apply=%region_5.0 | all-reduce | flops 1024 | bytes 8192 | tf_op jit(solution)/shard_map/psum | solution.py:40
  315.7 4.3 %fusion.20 = f32[1,1024]{1,0:T(1,128)S(1)} fusion(f32[1024,1]{0,1:T(1,128)S(1)} %bitcast.66, f32[1024,1024]{1,0:T(8,128)} %copy-done), kind=kOutput, calls=%fused_computation.42 | convolution fusion | flops 12582912 | bytes 4202496 | tf_op jit(solution)/shard_map/dot_general | solution.py:36
  319.9 62.7 %psum.53 = f32[1024]{0:T(1024)S(1)} all-reduce(f32[1024]{0:T(1024)S(1)} %bitcast.67), channel_id=1, replica_groups=mesh['cent'=8,'dp'=32] {'dp'}, use_global_device_ids=true, to_apply=%region_6.0 | all-reduce | flops 1024 | bytes 8192 | tf_op jit(solution)/shard_map/psum | solution.py:37
  382.6 5.8 %fusion.21 = f32[1,1024]{1,0:T(1,128)S(1)} fusion(f32[1024,1024]{1,0:T(8,128)} %copy-done, f32[1024,1]{0,1:T(1,128)S(1)} %bitcast.54), kind=kOutput, calls=%fused_computation.43 | convolution fusion | flops 12582912 | bytes 4202496 | tf_op jit(solution)/shard_map/dot_general | solution.py:38
  388.4 2.8 gather_fusion
  391.4 16.5 %all-reduce = (f32[1024]{0:T(1024)S(1)}, f32[1024]{0:T(1024)S(1)}) all-reduce(f32[1024]{0:T(1024)S(1)} %bitcast.60, f32[1024]{0:T(1024)S(1)} %reduce_sum.59), channel_id=1, replica_groups=mesh['cent'=8,'dp'=32] {'cent'}, use_global_device_ids=true, to_apply=%region_7.0 | all-reduce | flops 2048 | bytes 16384 | tf_op jit(solution)/shard_map/psum | solution.py:62
  407.9 4.0 multiply_convert_fusion
  (28 shorter events, 2.7 us)
Async XLA Ops:
  13.5 8.3 %copy-start.1 = (bf16[1024,1024]{1,0:T(8,128)(2,1)S(1)}, bf16[1024,1024]{1,0:T(8,128)(2,1)}, u32[]{:S(2)}) copy-start(bf16[1024,1024]{1,0:T(8,128)(2,1)} %param.4) | copy-start | bytes 6291460
  13.5 183.0 %all-to-all-start = ((bf16[32,128,1024]{2,1,0:T(8,128)(2,1)}), bf16[32,128,1024]{2,1,0:T(8,128)(2,1)}, u32[]{:S(2)}, u32[]{:S(2)}) async-start(bf16[32,128,1024]{2,1,0:T(8,128)(2,1)} %bitcast.51), calls=%async_computation | async-start | bytes 16777216 | tf_op jit(solution)/shard_map/all_to_all | solution.py:52
  19.6 2.7 copy-start.2
  24.9 1.9 copy-start
  26.9 169.4 %copy-start.3 = (bf16[2,128,1024]{2,1,0:T(8,128)(2,1)S(1)}, bf16[2,128,1024]{2,1,0:T(8,128)(2,1)}, u32[]{:S(2)}) copy-start(bf16[2,128,1024]{2,1,0:T(8,128)(2,1)} %param.7) | copy-start | bytes 1572868
  208.0 180.4 %all-to-all-start.1 = ((f32[32,128,128]{2,1,0:T(8,128)}), f32[32,128,128]{2,1,0:T(8,128)S(1)}, u32[]{:S(2)}, u32[]{:S(2)}) async-start(f32[32,128,128]{2,1,0:T(8,128)} %bitcast.53), calls=%async_computation.1 | async-start | bytes 4194304 | tf_op jit(solution)/shard_map/all_to_all | solution.py:58
where the time goes:
time: 414 us; the launch traced here: 413 us
  blocking collectives  333 us (80%)
  matrix products  36.6 us (9%)
  local copies, waits for them, and re-layouts  17.1 us (4%)
  other arithmetic  13.9 us (3%)
  starting transfers between devices  11.5 us (3%)
    psum x3, blocking collectives, shards(): col_scale = 1.0 / lax.psum(col_part, 'dp')  282 us
    psum x2, blocking collectives, shards(): row_scale = 1.0 / lax.psum(row_part, 'cent')  34.2 us
    dot_general x3, matrix products, shards(): row_part = jnp.dot(expo, col_scale, precision=lax.Precision.HIGHEST)  17.3 us
    psum x1, blocking collectives, shards(): row_total = lax.psum(row_part, 'cent')  16.5 us
    scatter x1, local copies, waits for them, and re-layouts, shards(): jnp.zeros((clusters * CAP, width), jnp.bfloat16).at[slot].set(points)  10.8 us
    dot_general x3, matrix products, shards(): col_part = jnp.dot(row_scale, expo, precision=lax.Precision.HIGHEST)  10.6 us
  transfers between devices with their start and end apart: 2, of which 0 were waited for; matrix products, arithmetic and copies ran while one was open for 8% of the time, Pallas kernels for 0%

commit v1 on v0

--- a/solution.py
+++ b/solution.py
@@ -37,7 +37,7 @@
         col_scale = 1.0 / lax.psum(col_part, "dp")
         row_part = jnp.dot(expo, col_scale, precision=lax.Precision.HIGHEST)
         if step + 1 < ITERS:
-            row_scale = 1.0 / lax.psum(row_part, "cent")
+            row_scale = 1.0 / jnp.sum(lax.all_gather(row_part, "cent"), axis=0)
     ids = cluster_ids[:, 0]
     labels = lax.broadcasted_iota(jnp.int32, (pts_count, clusters), 1)
     onehot = ids[:, None] == labels

time: 414 us -> 433 us (1.046)
  blocking collectives: 333 us -> 352 us
    all_gather x0 -> x2, blocking collectives: none -> 53 us  [shards(): row_scale = 1.0 / jnp.sum(lax.all_gather(row_part, 'cent'), axis=0)]
    psum x2 -> x0, blocking collectives: 34.2 us -> none  [shards(): row_scale = 1.0 / lax.psum(row_part, 'cent')]
where the time goes in v1:
time: 433 us; the launch traced here: 432 us
  blocking collectives  352 us (81%)
  matrix products  36.6 us (8%)
  local copies, waits for them, and re-layouts  17.1 us (4%)
  other arithmetic  13.9 us (3%)
  starting transfers between devices  11.2 us (3%)
    psum x3, blocking collectives, shards(): col_scale = 1.0 / lax.psum(col_part, 'dp')  283 us
    all_gather x2, blocking collectives, shards(): row_scale = 1.0 / jnp.sum(lax.all_gather(row_part, 'cent'), axis=0)  53 us
    dot_general x3, matrix products, shards(): row_part = jnp.dot(expo, col_scale, precision=lax.Precision.HIGHEST)  17.3 us
    psum x1, blocking collectives, shards(): row_total = lax.psum(row_part, 'cent')  16.6 us
    scatter x1, local copies, waits for them, and re-layouts, shards(): jnp.zeros((clusters * CAP, width), jnp.bfloat16).at[slot].set(points)  10.8 us
    dot_general x3, matrix products, shards(): col_part = jnp.dot(row_scale, expo, precision=lax.Precision.HIGHEST)  10.6 us
  transfers between devices with their start and end apart: 2, of which 0 were waited for; matrix products, arithmetic and copies ran while one was open for 8% of the time, Pallas kernels for 0%

profile of v1, /device:TPU:0, one launch (start us, length us, event | category | flops | bytes accessed | tf_op | source)
XLA Modules:
  0.0 431.9 jit_solution(11032764606834018619)
XLA Ops:
  0.6 1.4 fusion.11
  2.7 10.8 %scatter_custom_fusion = bf16[4096,1024]{1,0:T(8,128)(2,1)} fusion(s32[1024]{0:T(1024)S(1)} %bitcast.56, bf16[1024,1024]{1,0:T(8,128)(2,1)} %param.4, bf16[]{:T(256)} %constant.6.clone.1), kind=kCustom, calls=%fused_computation.6 | custom fusion | bytes 8389120 | tf_op jit(solution)/shard_map/scatter | solution.py:49
  13.5 6.1 %all-to-all-start = ((bf16[32,128,1024]{2,1,0:T(8,128)(2,1)}), bf16[32,128,1024]{2,1,0:T(8,128)(2,1)}, u32[]{:S(2)}, u32[]{:S(2)}) async-start(bf16[32,128,1024]{2,1,0:T(8,128)(2,1)} %bitcast.51), calls=%async_computation | async-start | bytes 16777216 | tf_op jit(solution)/shard_map/all_to_all | solution.py:52
  19.6 2.2 multiply_reduce_fusion.1
  22.3 2.6 multiply_exponential_fusion
  24.9 1.9 copy-done
  26.9 2.1 fusion.14
  28.9 141.6 %psum.35 = f32[1024]{0:T(1024)S(1)} all-reduce(f32[1024]{0:T(1024)S(1)} %bitcast.55), channel_id=1, replica_groups=mesh['cent'=8,'dp'=32] {'dp'}, use_global_device_ids=true, to_apply=%region_2.0 | all-reduce | flops 1024 | bytes 8192 | tf_op jit(solution)/shard_map/psum | solution.py:37
  170.5 5.8 %fusion.17 = f32[1,1024]{1,0:T(1,128)S(1)} fusion(f32[1024,1024]{1,0:T(8,128)} %copy-done, f32[1024,1]{0,1:T(1,128)S(1)} %bitcast.63), kind=kOutput, calls=%fused_computation.39 | convolution fusion | flops 12582912 | bytes 4202496 | tf_op jit(solution)/shard_map/dot_general | solution.py:38
  176.3 28.3 %all-gather = f32[8192]{0:T(1024)S(1)} all-gather(f32[1024]{0:T(1024)S(1)} %bitcast.59), channel_id=2, replica_groups=mesh['cent'=8,'dp'=32] {'cent'}, dimensions={0}, use_global_device_ids=true | all-gather | bytes 36864 | tf_op jit(solution)/shard_map/all_gather | solution.py:40
  204.9 5.1 %multiply_reduce_fusion = f32[32,128]{1,0:T(8,128)S(1)} fusion(bf16[32,128,1024]{2,1,0:T(8,128)(2,1)} %all-to-all-done), kind=kLoop, calls=%fused_computation.2 | loop fusion | flops 12578816 | bytes 8404992 | tf_op jit(solution)/shard_map/reduce_sum | solution.py:14
  210.1 4.8 %fusion.7 = f32[32,2,64,128]{3,2,0,1:T(8,128)S(1)} fusion(bf16[32,2,64,1024]{3,2,1,0:T(8,128)(2,1)} %bitcast.16, f32[2,128]{1,0:T(2,128)S(1)} %add_rsqrt_fusion.3, f32[32,2,64]{2,0,1:T(8,128)S(1)} %copy.13, bf16[2,128,1024]{2,1,0:T(8,128)(2,1)S(1)} %copy-done.3), kind=kOutput, calls=%fused_computation.16 | convolution fusion | flops 1075314688 | bytes 11027456 | tf_op jit(solution)/shard_map/sgcd,gkd->sgck/dot_general | solution.py:55
  214.8 1.5 copy.14
  216.3 5.2 %all-to-all-start.1 = ((f32[32,128,128]{2,1,0:T(8,128)}), f32[32,128,128]{2,1,0:T(8,128)S(1)}, u32[]{:S(2)}, u32[]{:S(2)}) async-start(f32[32,128,128]{2,1,0:T(8,128)} %bitcast.53), calls=%async_computation.1 | async-start | bytes 4194304 | tf_op jit(solution)/shard_map/all_to_all | solution.py:58
  221.5 4.3 fusion.18
  225.8 78.3 %psum.36 = f32[1024]{0:T(1024)S(1)} all-reduce(f32[1024]{0:T(1024)S(1)} %bitcast.64), channel_id=1, replica_groups=mesh['cent'=8,'dp'=32] {'dp'}, use_global_device_ids=true, to_apply=%region_4.0 | all-reduce | flops 1024 | bytes 8192 | tf_op jit(solution)/shard_map/psum | solution.py:37
  304.1 5.8 %fusion.19 = f32[1,1024]{1,0:T(1,128)S(1)} fusion(f32[1024,1024]{1,0:T(8,128)} %copy-done, f32[1024,1]{0,1:T(1,128)S(1)} %bitcast.65), kind=kOutput, calls=%fused_computation.41 | convolution fusion | flops 12582912 | bytes 4202496 | tf_op jit(solution)/shard_map/dot_general | solution.py:38
  309.8 24.7 %all-gather.1 = f32[8192]{0:T(1024)S(1)} all-gather(f32[1024]{0:T(1024)S(1)} %bitcast.60), channel_id=3, replica_groups=mesh['cent'=8,'dp'=32] {'cent'}, dimensions={0}, use_global_device_ids=true | all-gather | bytes 36864 | tf_op jit(solution)/shard_map/all_gather | solution.py:40
  334.5 4.3 fusion.20
  338.8 62.7 %psum.37 = f32[1024]{0:T(1024)S(1)} all-reduce(f32[1024]{0:T(1024)S(1)} %bitcast.67), channel_id=1, replica_groups=mesh['cent'=8,'dp'=32] {'dp'}, use_global_device_ids=true, to_apply=%region_6.0 | all-reduce | flops 1024 | bytes 8192 | tf_op jit(solution)/shard_map/psum | solution.py:37
  401.5 5.8 %fusion.21 = f32[1,1024]{1,0:T(1,128)S(1)} fusion(f32[1024,1024]{1,0:T(8,128)} %copy-done, f32[1024,1]{0,1:T(1,128)S(1)} %bitcast.54), kind=kOutput, calls=%fused_computation.43 | convolution fusion | flops 12582912 | bytes 4202496 | tf_op jit(solution)/shard_map/dot_general | solution.py:38
  407.2 2.8 gather_fusion
  410.3 16.6 %all-reduce = (f32[1024]{0:T(1024)S(1)}, f32[1024]{0:T(1024)S(1)}) all-reduce(f32[1024]{0:T(1024)S(1)} %bitcast.62, f32[1024]{0:T(1024)S(1)} %reduce_sum.79), channel_id=1, replica_groups=mesh['cent'=8,'dp'=32] {'cent'}, use_global_device_ids=true, to_apply=%region_7.0 | all-reduce | flops 2048 | bytes 16384 | tf_op jit(solution)/shard_map/psum | solution.py:62
  426.9 4.0 multiply_convert_fusion
  (32 shorter events, 2.7 us)
Async XLA Ops:
  13.5 8.3 %copy-start.1 = (bf16[1024,1024]{1,0:T(8,128)(2,1)S(1)}, bf16[1024,1024]{1,0:T(8,128)(2,1)}, u32[]{:S(2)}) copy-start(bf16[1024,1024]{1,0:T(8,128)(2,1)} %param.4) | copy-start | bytes 6291460
  13.5 191.4 %all-to-all-start = ((bf16[32,128,1024]{2,1,0:T(8,128)(2,1)}), bf16[32,128,1024]{2,1,0:T(8,128)(2,1)}, u32[]{:S(2)}, u32[]{:S(2)}) async-start(bf16[32,128,1024]{2,1,0:T(8,128)(2,1)} %bitcast.51), calls=%async_computation | async-start | bytes 16777216 | tf_op jit(solution)/shard_map/all_to_all | solution.py:52
  19.6 2.7 copy-start.2
  24.9 1.9 copy-start
  26.9 177.8 %copy-start.3 = (bf16[2,128,1024]{2,1,0:T(8,128)(2,1)S(1)}, bf16[2,128,1024]{2,1,0:T(8,128)(2,1)}, u32[]{:S(2)}) copy-start(bf16[2,128,1024]{2,1,0:T(8,128)(2,1)} %param.7) | copy-start | bytes 1572868
  216.3 190.9 %all-to-all-start.1 = ((f32[32,128,128]{2,1,0:T(8,128)}), f32[32,128,128]{2,1,0:T(8,128)S(1)}, u32[]{:S(2)}, u32[]{:S(2)}) async-start(f32[32,128,128]{2,1,0:T(8,128)} %bitcast.53), calls=%async_computation.1 | async-start | bytes 4194304 | tf_op jit(solution)/shard_map/all_to_all | solution.py:58
